TPU v7x, 256 devices: a whole 4x4x8 slice. The times are simulated.
256 devices in a mesh: ctx: 4 (over y), exp: 64 (over z, x, core).
Axes of the slice: x: 4, y: 4, z: 8, core: 2. Of those that a mesh axis runs over, the one named last changes fastest.
Arguments:
- residual_in: bfloat16 [64, 256, 1536], P('exp', 'ctx'), may hold values from -6 to 6
- queries: bfloat16 [64, 256, 1536], P('exp', 'ctx'), may hold values from -6 to 6
- new_kv: bfloat16 [64, 256, 1024], P('exp', 'ctx'), may hold values from -6 to 6
- cache_kv: bfloat16 [64, 4096, 1024], P('exp', 'ctx'), may hold values from -6 to 6
- cache_len: int32 [64], P('exp'), may hold values from 1 to 4096, 133120 in all
- out_proj: bfloat16 [1536, 1536], replicated, may hold values from -0.625 to 0.625
- norm_gain: float32 [1536], replicated, may hold values from 0.1 to 1.9
- routes: int32 [64, 256, 6], P('exp', 'ctx'), may hold values from 0 to 63, all different within a row; in each aligned block of 64 rows (0 to 63, 64 to 127, ..., all dimensions but the last counted through in order) at most 9 rows name the same one
- route_w: bfloat16 [64, 256, 6], P('exp', 'ctx'), may hold values from 0.049804688 to 0.5
- w_gate_up: bfloat16 [64, 1536, 1024], P('exp'), may hold values from -0.15625 to 0.15625
- w_down: bfloat16 [64, 512, 1536], P('exp'), may hold values from -0.25 to 0.25
Outputs:
- layer_out: bfloat16 [64, 256, 1536], P('exp', 'ctx')
Inputs may be any that keep to these rules, and one draw needn't show every extreme that they name: `cache_len`: the largest length is exactly 4096. `routes`: each token names 6 different experts; among the new tokens of one device (aligned blocks of 64 tokens) no expert is named by more than 9 tokens, a bound that some block reaches.
All inputs are finite; a program needn't handle non-finite values. No bound on the sum of `cache_len` on one device may be relied on, other than what follows from the above.
Results may differ from a plain program's by a relative error of at most 0.02.
Values may be sent and summed in bfloat16 or wider, within the bound.
No kernel may reach another device: no remote copies, remote signals or barrier semaphores. Data moves between devices by JAX's collectives and lax.ppermute only.
A program may use at most 128 MiB of HBM per device.

v0:
```python
import jax
import jax.numpy as jnp
from jax import lax
from jax.sharding import PartitionSpec as P

D = 1536
KVH = 4
HD = 128
GROUP = 3
NEG_BIG = -1e30


def local(
    residual_in,
    queries,
    new_kv,
    cache_kv,
    cache_len,
    out_proj,
    norm_gain,
    routes,
    route_w,
    w_gate_up,
    w_down,
):
    tok_count = residual_in.shape[1]
    cache_rows = cache_kv.shape[1]
    n_ctx = lax.axis_size("ctx")
    ctx_pos = lax.axis_index("ctx")
    length = cache_len[0]
    score_scale = HD ** (-0.5)
    heads = KVH * GROUP
    all_queries = lax.all_gather(queries[0], "ctx", axis=0, tiled=True)
    query_total = all_queries.shape[0]
    query_grid = all_queries.reshape(query_total, KVH, GROUP, HD)
    local_keys = jnp.concatenate([cache_kv[0], new_kv[0]], 0)
    key_rows = local_keys.shape[0]
    key_width = local_keys.shape[1] // 2
    key_part = local_keys[:, :key_width].reshape(key_rows, KVH, HD)
    value_part = local_keys[:, key_width:].reshape(key_rows, KVH, HD)
    scores = (
        jnp.einsum("qkgd,rkd->kgqr", query_grid, key_part, preferred_element_type=jnp.float32)
        * score_scale
    )
    row_index = jnp.arange(key_rows)
    cached = row_index < cache_rows
    cache_pos = ctx_pos * cache_rows + row_index
    new_pos = ctx_pos * tok_count + row_index - cache_rows
    query_pos = jnp.arange(query_total)
    usable = jnp.where(
        cached[None, :], (cache_pos < length)[None, :], new_pos[None, :] <= query_pos[:, None]
    )
    part_max = jnp.max(jnp.where(usable, scores, NEG_BIG), -1)
    softmax_terms = jnp.where(usable, jnp.exp(scores - part_max[..., None]), 0.0)
    part_sum = jnp.sum(softmax_terms, -1)
    part_acc = jnp.einsum(
        "kgqr,rkd->qkgd",
        softmax_terms.astype(jnp.bfloat16),
        value_part,
        preferred_element_type=jnp.float32,
    )
    part_acc = part_acc.reshape(n_ctx, tok_count, heads, HD)
    stats = jnp.stack([part_max, part_sum], 0).reshape(2, heads, n_ctx, tok_count)
    stats = stats.transpose(2, 3, 1, 0).reshape(n_ctx, tok_count, heads * 2)
    got_acc = lax.all_to_all(part_acc, "ctx", split_axis=0, concat_axis=0, tiled=True)
    got_stats = lax.all_to_all(stats, "ctx", split_axis=0, concat_axis=0, tiled=True)
    got_stats = got_stats.reshape(n_ctx, tok_count, heads, 2)
    got_max = got_stats[..., 0]
    got_sum = got_stats[..., 1]
    top_max = jnp.max(got_max, 0)
    rescale = jnp.exp(got_max - top_max[None])
    total_sum = jnp.sum(rescale * got_sum, 0)
    total_acc = jnp.sum(rescale[..., None] * got_acc, 0)
    attended = (total_acc / total_sum[..., None]).reshape(tok_count, heads * HD)
    attended = attended.astype(jnp.bfloat16)
    mixed = (
        residual_in[0].astype(jnp.float32)
        + jnp.dot(attended, out_proj, preferred_element_type=jnp.float32)
    ).astype(jnp.bfloat16)
    widened = mixed.astype(jnp.float32)
    normed = (
        widened * lax.rsqrt(jnp.mean(widened * widened, -1, keepdims=True) + 1e-06) * norm_gain
    ).astype(jnp.bfloat16)
    top_count = routes.shape[2]
    local_experts = w_gate_up.shape[0]
    expert_total = local_experts * lax.axis_size("exp")
    capacity = min(tok_count, 3 * tok_count * top_count // (2 * expert_total))
    expert_ids = routes[0].reshape(-1)
    one_hot = (expert_ids[:, None] == jnp.arange(expert_total)[None, :]).astype(jnp.int32)
    before = jnp.cumsum(one_hot, 0) - one_hot
    slot_index = jnp.sum(before * one_hot, 1)
    dest = (expert_ids * capacity + slot_index).reshape(tok_count, top_count)
    slot_ids = jnp.arange(expert_total * capacity)
    hits = dest[None, :, :] == slot_ids[:, None, None]
    select = jnp.any(hits, -1).astype(jnp.bfloat16)
    outgoing = jnp.dot(select, normed, preferred_element_type=jnp.float32).astype(jnp.bfloat16)
    outgoing = outgoing.reshape(expert_total, capacity, D)
    hidden_half = w_gate_up.shape[2] // 2
    incoming = lax.all_to_all(outgoing, "exp", split_axis=0, concat_axis=0, tiled=True)
    item_count = incoming.shape[1]
    grouped = incoming.reshape(-1, local_experts, item_count, incoming.shape[2])
    gate_up = jnp.einsum("sekd,edf->sekf", grouped, w_gate_up, preferred_element_type=jnp.float32)
    activated = (jax.nn.silu(gate_up[..., :hidden_half]) * gate_up[..., hidden_half:]).astype(
        jnp.bfloat16
    )
    result = jnp.einsum(
        "sekf,efd->sekd", activated, w_down, preferred_element_type=jnp.float32
    ).astype(jnp.bfloat16)
    returned = lax.all_to_all(
        result.reshape(incoming.shape), "exp", split_axis=0, concat_axis=0, tiled=True
    )
    weights = route_w[0]
    combine = jnp.sum(
        jnp.where(hits.transpose(1, 0, 2), weights[:, None, :], jnp.zeros((), weights.dtype)), -1
    )
    blended = jnp.dot(combine, returned.reshape(-1, D), preferred_element_type=jnp.float32)
    return (widened + blended).astype(jnp.bfloat16)[None]


def solution(mesh):
    return jax.shard_map(
        local,
        mesh=mesh,
        in_specs=(
            P("exp", "ctx", None),
            P("exp", "ctx", None),
            P("exp", "ctx", None),
            P("exp", "ctx", None),
            P("exp"),
            P(),
            P(),
            P("exp", "ctx", None),
            P("exp", "ctx", None),
            P("exp", None, None),
            P("exp", None, None),
        ),
        out_specs=P("exp", "ctx", None),
        check_vma=False,
    )
```

profile of v0, /device:TPU:2, one launch (start us, length us, event | category | flops | bytes accessed | tf_op | source)
XLA Modules:
  0.0 276.0 jit_solution(6451135125738383920)
XLA Ops:
  0.8 3.2 %fusion.25 = (bf16[1088,512]{1,0:T(8,128)(2,1)}, bf16[1088,512]{1,0:T(8,128)(2,1)}) fusion(bf16[1024,1024]{1,0:T(8,128)(2,1)} %bitcast.119, bf16[64,1024]{1,0:T(8,128)(2,1)} %bitcast.123), kind=kLoop, calls=%fused_computation.28 | loop fusion | flops 4456448 | bytes 4456448 | tf_op jit(solution)/shard_map/concatenate | solution.py:36
  4.0 2.4 copy.119
  6.4 14.6 %all-gather = bf16[1,256,1536]{2,1,0:T(8,128)(2,1)} all-gather(bf16[1,64,1536]{2,1,0:T(8,128)(2,1)S(1)} %copy-done.1), channel_id=2, replica_groups=mesh['ctx'=4,'exp'=64] {'ctx'}, dimensions={1}, use_global_device_ids=true | all-gather | bytes 983040 | tf_op jit(solution)/shard_map/all_gather | solution.py:33
  21.0 2.3 copy.120
  24.2 8.5 %fusion = (f32[4,3,256]{2,1,0:T(4,128)S(1)}, f32[4,1088,256,3]{2,1,3,0:T(8,128)}) fusion(pred[256,1088]{0,1:T(8,128)(4,1)S(1)} %fusion.26, bf16[1088,4,128,1]{0,2,3,1:T(8,128)(2,1)} %bitcast.117, bf16[256,4,3,128]{0,3,2,1:T(8,128)(2,1)} %bitcast.118), kind=kOutput, calls=%fused_computation.2 | convolution fusion | flops 865661952 | bytes 15560704 | tf_op jit(solution)/shard_map/qkgd,rkd->kgqr/dot_general | solution.py:42
  32.8 7.5 %fusion.4 = f32[4,3,256]{2,1,0:T(4,128)S(1)} fusion(f32[4,1088,256,3]{2,1,3,0:T(8,128)} %get-tuple-element.11, f32[4,3,256]{2,1,0:T(4,128)S(1)} %get-tuple-element.10, pred[256,1088]{0,1:T(8,128)(4,1)S(1)} %fusion.26), kind=kLoop, calls=%fused_computation.6 | loop fusion | flops 13366272 | bytes 13672448 | tf_op jit(solution)/shard_map/reduce_sum | solution.py:55
  41.2 4.4 %all-to-all-start = ((f32[4,1,1536]{2,1,0:T(1,128)}), f32[4,1,1536]{2,1,0:T(1,128)S(1)}, u32[]{:S(2)}, u32[]{:S(2)}) async-start(f32[4,1,1536]{2,1,0:T(1,128)} %reshape.117), calls=%async_computation | async-start | bytes 49152 | tf_op jit(solution)/shard_map/all_to_all | solution.py:66
  45.6 2.4 copy.126
  47.9 9.1 %fusion.21 = f32[256,4,3,128]{0,3,2,1:T(8,128)} fusion(bf16[1088,4,128,1]{0,2,3,1:T(8,128)(2,1)} %bitcast.120, f32[4,1088,256,3]{2,1,3,0:T(8,128)} %get-tuple-element.11, f32[4,3,256]{2,1,0:T(4,128)S(1)} %get-tuple-element.10, pred[256,1088]{0,1:T(8,128)(4,1)S(1)} %fusion.26), kind=kOutput, calls=%fused_computation.25 | convolution fusion | flops 869007360 | bytes 16347136 | tf_op jit(solution)/shard_map/kgqr,rkd->qkgd/dot_general | solution.py:56
  57.1 3.0 %copy.128 = f32[256,4,3,128]{3,0,2,1:T(8,128)} copy(f32[256,4,3,128]{0,3,2,1:T(8,128)} %fusion.21) | data formatting | bytes 3145728 | tf_op jit(solution)/shard_map/kgqr,rkd->qkgd/transpose | solution.py:56
  60.1 2.8 copy.129
  63.1 4.8 %all-to-all-start.1 = ((f32[4,64,12,128]{3,1,2,0:T(8,128)}), f32[4,64,12,128]{3,1,2,0:T(8,128)}, u32[]{:S(2)}, u32[]{:S(2)}) async-start(f32[4,64,12,128]{3,1,2,0:T(8,128)} %copy.129), calls=%async_computation.1 | async-start | bytes 3145728 | tf_op jit(solution)/shard_map/all_to_all | solution.py:65
  71.8 14.0 %all-to-all-done.1 = f32[4,64,12,128]{3,1,2,0:T(8,128)} async-done(((f32[4,64,12,128]{3,1,2,0:T(8,128)}), f32[4,64,12,128]{3,1,2,0:T(8,128)}, u32[]{:S(2)}, u32[]{:S(2)}) %all-to-all-start.1) | async-done | bytes 1572896 | tf_op jit(solution)/shard_map/all_to_all | solution.py:65
  85.7 1.9 multiply_reduce_fusion
  87.7 3.5 %multiply_reduce_fusion.1 = (f32[64]{0:T(128)S(1)}, f32[64,1536]{1,0:T(8,128)S(1)}) fusion(bf16[1536,1536]{1,0:T(8,128)(2,1)} %param.16, bf16[1,64,1536]{2,1,0:T(8,128)(2,1)} %param.11, f32[64,12,128]{2,0,1:T(8,128)S(1)} %multiply_reduce_fusion, f32[64,12]{0,1:T(8,128)S(1)} %fusion.41), kind=kOutput, calls=%fused_computation.39 | convolution fusion | flops 302776256 | bytes 5704960 | tf_op jit(solution)/shard_map/dot_general | solution.py:78
  91.1 1.9 convolution_convert_fusion
  93.1 4.2 %reshape.104 = bf16[64,9,1536]{2,1,0:T(8,128)(2,1)} reshape(bf16[576,1536]{1,0:T(8,128)(2,1)} %convolution_convert_fusion) | data formatting | bytes 3538944 | tf_op jit(solution)/shard_map/reshape | solution.py:97
  97.2 85.7 %all_to_all.20 = bf16[64,9,1536]{2,1,0:T(8,128)(2,1)S(1)} all-to-all(bf16[64,9,1536]{2,1,0:T(8,128)(2,1)} %reshape.104), channel_id=1, replica_groups=mesh['ctx'=4,'exp'=64] {'exp'}, dimensions={0} | all-to-all | bytes 3538944 | tf_op jit(solution)/shard_map/all_to_all | solution.py:99
  183.0 2.5 fusion.15
  186.6 2.8 %copy.138 = bf16[64,9,1536]{2,1,0:T(8,128)(2,1)} copy(bf16[64,9,1536]{2,0,1:T(8,128)(2,1)S(1)} %convolution_convert_fusion.1) | data formatting | bytes 3538944 | tf_op jit(solution)/shard_map/convert_element_type | solution.py:108
  189.4 6.0 %all-to-all-start.3 = ((bf16[64,9,1536]{2,1,0:T(8,128)(2,1)}), bf16[64,9,1536]{2,1,0:T(8,128)(2,1)}, u32[]{:S(2)}, u32[]{:S(2)}) async-start(bf16[64,9,1536]{2,1,0:T(8,128)(2,1)} %copy.138), calls=%async_computation.3 | async-start | bytes 6291456 | tf_op jit(solution)/shard_map/all_to_all | solution.py:109
  196.2 72.8 %all-to-all-done.3 = bf16[64,9,1536]{2,1,0:T(8,128)(2,1)} async-done(((bf16[64,9,1536]{2,1,0:T(8,128)(2,1)}), bf16[64,9,1536]{2,1,0:T(8,128)(2,1)}, u32[]{:S(2)}, u32[]{:S(2)}) %all-to-all-start.3) | async-done | bytes 1769504 | tf_op jit(solution)/shard_map/all_to_all | solution.py:109
  269.1 4.2 %reshape.108 = bf16[576,1536]{1,0:T(8,128)(2,1)} reshape(bf16[64,9,1536]{2,1,0:T(8,128)(2,1)} %all-to-all-done.3) | data formatting | bytes 3538944 | tf_op jit(solution)/shard_map/reshape | solution.py:116
  273.3 2.7 fusion.13
  (46 shorter events, 7.8 us)
Async XLA Ops:
  0.0 183.0 %copy-start = (bf16[1,1536,1024]{2,1,0:T(8,128)(2,1)S(1)}, bf16[1,1536,1024]{2,1,0:T(8,128)(2,1)}, u32[]{:S(2)}) copy-start(bf16[1,1536,1024]{2,1,0:T(8,128)(2,1)} %param.20) | copy-start | bytes 9437188
  4.0 2.4 copy-start.1
  41.2 21.9 %all-to-all-start = ((f32[4,1,1536]{2,1,0:T(1,128)}), f32[4,1,1536]{2,1,0:T(1,128)S(1)}, u32[]{:S(2)}, u32[]{:S(2)}) async-start(f32[4,1,1536]{2,1,0:T(1,128)} %reshape.117), calls=%async_computation | async-start | bytes 49152 | tf_op jit(solution)/shard_map/all_to_all | solution.py:66
  60.1 2.8 copy-start.3
  63.1 22.6 %all-to-all-start.1 = ((f32[4,64,12,128]{3,1,2,0:T(8,128)}), f32[4,64,12,128]{3,1,2,0:T(8,128)}, u32[]{:S(2)}, u32[]{:S(2)}) async-start(f32[4,64,12,128]{3,1,2,0:T(8,128)} %copy.129), calls=%async_computation.1 | async-start | bytes 3145728 | tf_op jit(solution)/shard_map/all_to_all | solution.py:65
  87.6 3.5 %copy-start.2 = (pred[576,64]{0,1:T(8,128)(4,1)S(1)}, pred[576,64]{0,1:T(8,128)(4,1)}, u32[]{:S(2)}) copy-start(pred[576,64]{0,1:T(8,128)(4,1)} %fusion.28) | copy-start | bytes 110596
  87.6 3.5 %copy-start.4 = (f32[1536]{0:T(1024)S(1)}, f32[1536]{0:T(1024)}, u32[]{:S(2)}) copy-start(f32[1536]{0:T(1024)} %param.17) | copy-start | bytes 18436
  183.0 2.5 copy-start.6
  189.4 6.0 %copy-start.5 = (bf16[1,64,6]{1,2,0:T(8,128)(2,1)S(1)}, bf16[1,64,6]{1,2,0:T(8,128)(2,1)}, u32[]{:S(2)}) copy-start(bf16[1,64,6]{1,2,0:T(8,128)(2,1)} %param.19) | copy-start | bytes 2308
  189.4 79.6 %all-to-all-start.3 = ((bf16[64,9,1536]{2,1,0:T(8,128)(2,1)}), bf16[64,9,1536]{2,1,0:T(8,128)(2,1)}, u32[]{:S(2)}, u32[]{:S(2)}) async-start(bf16[64,9,1536]{2,1,0:T(8,128)(2,1)} %copy.138), calls=%async_computation.3 | async-start | bytes 6291456 | tf_op jit(solution)/shard_map/all_to_all | solution.py:109
where the time goes:
time: 277 us; the launch traced here: 276 us
  blocking collectives  100 us (36%)
  waiting for transfers between devices  86.8 us (31%)
  matrix products  29.3 us (11%)
  local copies, waits for them, and re-layouts  26.4 us (10%)
  other arithmetic  17 us (6%)
  starting transfers between devices  15.2 us (5%)
    all_to_all x1, blocking collectives, local(): lax.all_to_all(outgoing, 'exp', split_axis=0, concat_axis=0, tiled=True)  85.7 us
    all_to_all x1, waiting for transfers between devices, local(): lax.all_to_all(result.reshape(incoming.shape), 'exp', split_axis=0, conca...  72.8 us
    all_gather x1, blocking collectives, local(): all_queries = lax.all_gather(queries[0], 'ctx', axis=0, tiled=True)  14.6 us
    all_to_all x1, waiting for transfers between devices, local(): lax.all_to_all(part_acc, 'ctx', split_axis=0, concat_axis=0, tiled=True)  14 us
    dot_general x1, matrix products, local(): jnp.einsum('kgqr,rkd->qkgd', softmax_terms.astype(jnp.bfloat16), value_pa...  9.13 us
    dot_general x1, matrix products, local(): jnp.einsum('qkgd,rkd->kgqr', query_grid, key_part, preferred_element_type...  8.52 us
    reduce_sum x1, other arithmetic, local(): part_sum = jnp.sum(softmax_terms, -1)  7.48 us
    all_to_all x1, starting transfers between devices, local(): lax.all_to_all(result.reshape(incoming.shape), 'exp', split_axis=0, conca...  5.97 us
  transfers between devices with their start and end apart: 3, of which 2 were waited for; matrix products, arithmetic and copies ran while one was open for 8% of the time, Pallas kernels for 0%

commit v1 on v0

--- a/solution.py
+++ b/solution.py
@@ -30,7 +30,9 @@
     length = cache_len[0]
     score_scale = HD ** (-0.5)
     heads = KVH * GROUP
-    all_queries = lax.all_gather(queries[0], "ctx", axis=0, tiled=True)
+    all_queries = jnp.concatenate(
+        lax.all_to_all(jnp.stack([queries[0]] * lax.axis_size("ctx")), "ctx", 0, 0), axis=0
+    )
     query_total = all_queries.shape[0]
     query_grid = all_queries.reshape(query_total, KVH, GROUP, HD)
     local_keys = jnp.concatenate([cache_kv[0], new_kv[0]], 0)

time: 277 us -> 274 us (0.989)
  blocking collectives: 100 us -> 85.7 us
  waiting for transfers between devices: 86.8 us -> 91.3 us
  local copies, waits for them, and re-layouts: 26.4 us -> 29.7 us
  starting transfers between devices: 15.2 us -> 18.4 us
    all_gather x1 -> x0, blocking collectives: 14.6 us -> none  [local(): all_queries = lax.all_gather(queries[0], 'ctx', axis=0, tiled=True)]
    another operation x0 -> x2, local copies, waits for them, and re-layouts: none -> 5.59 us  [the longest x1 3.57 us: local(): query_grid = all_queries.reshape(query_total, KVH, GROUP, HD)]
    all_to_all x0 -> x1, starting transfers between devices: none -> 4.46 us  [local(): lax.all_to_all(jnp.stack([queries[0]] * lax.axis_size('ctx')), 'ctx', 0, 0)]
  transfers between devices with their start and end apart: 3 -> 4, of which waited for: 2 -> 3; matrix products, arithmetic and copies ran while one was open for 8% -> 10% of each run, Pallas kernels for 0% -> 0%
where the time goes in v1:
time: 274 us; the launch traced here: 273 us
  waiting for transfers between devices  91.3 us (33%)
  blocking collectives  85.7 us (31%)
  local copies, waits for them, and re-layouts  29.7 us (11%)
  matrix products  29.7 us (11%)
  starting transfers between devices  18.4 us (7%)
  other arithmetic  16.9 us (6%)
    all_to_all x1, blocking collectives, local(): lax.all_to_all(outgoing, 'exp', split_axis=0, concat_axis=0, tiled=True)  85.7 us
    all_to_all x1, waiting for transfers between devices, local(): lax.all_to_all(result.reshape(incoming.shape), 'exp', split_axis=0, conca...  72.8 us
    all_to_all x1, waiting for transfers between devices, local(): lax.all_to_all(part_acc, 'ctx', split_axis=0, concat_axis=0, tiled=True)  15.8 us
    dot_general x1, matrix products, local(): jnp.einsum('kgqr,rkd->qkgd', softmax_terms.astype(jnp.bfloat16), value_pa...  9.14 us
    dot_general x1, matrix products, local(): jnp.einsum('qkgd,rkd->kgqr', query_grid, key_part, preferred_element_type...  8.92 us
    reduce_sum x1, other arithmetic, local(): part_sum = jnp.sum(softmax_terms, -1)  7.48 us
    all_to_all x1, starting transfers between devices, local(): lax.all_to_all(result.reshape(incoming.shape), 'exp', split_axis=0, conca...  5.97 us
  transfers between devices with their start and end apart: 4, of which 3 were waited for; matrix products, arithmetic and copies ran while one was open for 10% of the time, Pallas kernels for 0%

profile of v1, /device:TPU:2, one launch (start us, length us, event | category | flops | bytes accessed | tf_op | source)
XLA Modules:
  0.0 272.6 jit_solution(530043840084113315)
XLA Ops:
  0.0 2.0 stack.12
  2.0 4.5 %all-to-all-start = ((bf16[4,64,1536]{2,1,0:T(8,128)(2,1)}), bf16[4,64,1536]{2,1,0:T(8,128)(2,1)}, u32[]{:S(2)}, u32[]{:S(2)}) async-start(bf16[4,64,1536]{2,1,0:T(8,128)(2,1)} %stack.12), calls=%async_computation | async-start | bytes 1572864 | tf_op jit(solution)/shard_map/all_to_all | solution.py:34
  7.2 3.1 %fusion.25 = (bf16[1088,512]{1,0:T(8,128)(2,1)}, bf16[1088,512]{1,0:T(8,128)(2,1)}) fusion(bf16[1024,1024]{1,0:T(8,128)(2,1)} %bitcast.117, bf16[64,1024]{1,0:T(8,128)(2,1)S(1)} %bitcast.122), kind=kLoop, calls=%fused_computation.28 | loop fusion | flops 4456448 | bytes 4456448 | tf_op jit(solution)/shard_map/concatenate | solution.py:38
  10.3 2.4 copy.114
  12.6 2.4 copy.120
  16.2 2.7 all-to-all-done
  18.9 3.6 %reshape_reshape.3 = bf16[256,4,3,128]{3,2,1,0:T(4,128)(2,1)} reshape(bf16[4,64,1536]{2,1,0:T(8,128)(2,1)} %all-to-all-done) | data formatting | bytes 1572864 | tf_op jit(solution)/shard_map/reshape;reshape | solution.py:37
  22.5 8.9 %fusion = (f32[4,3,256]{2,1,0:T(4,128)S(1)}, f32[4,1088,256,3]{2,1,3,0:T(8,128)}) fusion(pred[256,1088]{0,1:T(8,128)(4,1)S(1)} %fusion.26, bf16[1088,4,128,1]{0,2,3,1:T(8,128)(2,1)} %bitcast.116, bf16[256,4,3,128]{3,2,1,0:T(4,128)(2,1)} %reshape_reshape.3), kind=kOutput, calls=%fused_computation.2 | convolution fusion | flops 865661952 | bytes 15560704 | tf_op jit(solution)/shard_map/qkgd,rkd->kgqr/dot_general | solution.py:44
  31.5 7.5 %fusion.4 = f32[4,3,256]{2,1,0:T(4,128)S(1)} fusion(f32[4,1088,256,3]{2,1,3,0:T(8,128)} %get-tuple-element.11, f32[4,3,256]{2,1,0:T(4,128)S(1)} %get-tuple-element.10, pred[256,1088]{0,1:T(8,128)(4,1)S(1)} %fusion.26), kind=kLoop, calls=%fused_computation.6 | loop fusion | flops 13366272 | bytes 13672448 | tf_op jit(solution)/shard_map/reduce_sum | solution.py:57
  39.8 3.3 %all-to-all-start.1 = ((f32[4,1,1536]{2,1,0:T(1,128)}), f32[4,1,1536]{2,1,0:T(1,128)S(1)}, u32[]{:S(2)}, u32[]{:S(2)}) async-start(f32[4,1,1536]{2,1,0:T(1,128)} %reshape.112), calls=%async_computation.1 | async-start | bytes 49152 | tf_op jit(solution)/shard_map/all_to_all | solution.py:68
  43.1 9.1 %fusion.21 = f32[256,4,3,128]{0,3,2,1:T(8,128)} fusion(bf16[1088,4,128,1]{0,2,3,1:T(8,128)(2,1)} %bitcast.118, f32[4,1088,256,3]{2,1,3,0:T(8,128)} %get-tuple-element.11, f32[4,3,256]{2,1,0:T(4,128)S(1)} %get-tuple-element.10, pred[256,1088]{0,1:T(8,128)(4,1)S(1)} %fusion.26), kind=kOutput, calls=%fused_computation.25 | convolution fusion | flops 869007360 | bytes 16347136 | tf_op jit(solution)/shard_map/kgqr,rkd->qkgd/dot_general | solution.py:58
  52.2 3.0 %copy.122 = f32[256,4,3,128]{3,0,2,1:T(8,128)} copy(f32[256,4,3,128]{0,3,2,1:T(8,128)} %fusion.21) | data formatting | bytes 3145728 | tf_op jit(solution)/shard_map/kgqr,rkd->qkgd/transpose | solution.py:58
  55.2 2.7 %copy.123 = f32[4,64,12,128]{3,1,2,0:T(8,128)} copy(f32[4,64,12,128]{3,1,0,2:T(8,128)} %bitcast.115) | data formatting | bytes 3145728 | tf_op jit(solution)/shard_map/reshape | solution.py:64
  58.0 4.8 %all-to-all-start.2 = ((f32[4,64,12,128]{3,1,2,0:T(8,128)}), f32[4,64,12,128]{3,1,2,0:T(8,128)}, u32[]{:S(2)}, u32[]{:S(2)}) async-start(f32[4,64,12,128]{3,1,2,0:T(8,128)} %copy.123), calls=%async_computation.2 | async-start | bytes 3145728 | tf_op jit(solution)/shard_map/all_to_all | solution.py:67
  66.6 15.8 %all-to-all-done.2 = f32[4,64,12,128]{3,1,2,0:T(8,128)} async-done(((f32[4,64,12,128]{3,1,2,0:T(8,128)}), f32[4,64,12,128]{3,1,2,0:T(8,128)}, u32[]{:S(2)}, u32[]{:S(2)}) %all-to-all-start.2) | async-done | bytes 1572896 | tf_op jit(solution)/shard_map/all_to_all | solution.py:67
  84.3 3.5 %multiply_reduce_fusion.1 = (f32[64]{0:T(128)S(1)}, f32[64,1536]{1,0:T(8,128)S(1)}) fusion(bf16[1536,1536]{1,0:T(8,128)(2,1)} %param.16, bf16[1,64,1536]{2,1,0:T(8,128)(2,1)} %param.11, f32[64,12,128]{2,0,1:T(8,128)S(1)} %multiply_reduce_fusion, f32[64,12]{0,1:T(8,128)S(1)} %fusion.43), kind=kOutput, calls=%fused_computation.41 | convolution fusion | flops 302776256 | bytes 5704960 | tf_op jit(solution)/shard_map/dot_general | solution.py:80
  89.7 4.2 %reshape.101 = bf16[64,9,1536]{2,1,0:T(8,128)(2,1)} reshape(bf16[576,1536]{1,0:T(8,128)(2,1)} %convolution_convert_fusion) | data formatting | bytes 3538944 | tf_op jit(solution)/shard_map/reshape | solution.py:99
  93.9 85.7 %all_to_all.25 = bf16[64,9,1536]{2,1,0:T(8,128)(2,1)S(1)} all-to-all(bf16[64,9,1536]{2,1,0:T(8,128)(2,1)} %reshape.101), channel_id=1, replica_groups=mesh['ctx'=4,'exp'=64] {'exp'}, dimensions={0} | all-to-all | bytes 3538944 | tf_op jit(solution)/shard_map/all_to_all | solution.py:101
  179.6 2.5 fusion.15
  183.3 2.8 %copy.132 = bf16[64,9,1536]{2,1,0:T(8,128)(2,1)} copy(bf16[64,9,1536]{2,0,1:T(8,128)(2,1)S(1)} %convolution_convert_fusion.1) | data formatting | bytes 3538944 | tf_op jit(solution)/shard_map/convert_element_type | solution.py:110
  186.1 6.0 %all-to-all-start.4 = ((bf16[64,9,1536]{2,1,0:T(8,128)(2,1)}), bf16[64,9,1536]{2,1,0:T(8,128)(2,1)}, u32[]{:S(2)}, u32[]{:S(2)}) async-start(bf16[64,9,1536]{2,1,0:T(8,128)(2,1)} %copy.132), calls=%async_computation.4 | async-start | bytes 6291456 | tf_op jit(solution)/shard_map/all_to_all | solution.py:111
  192.9 72.8 %all-to-all-done.4 = bf16[64,9,1536]{2,1,0:T(8,128)(2,1)} async-done(((bf16[64,9,1536]{2,1,0:T(8,128)(2,1)}), bf16[64,9,1536]{2,1,0:T(8,128)(2,1)}, u32[]{:S(2)}, u32[]{:S(2)}) %all-to-all-start.4) | async-done | bytes 1769504 | tf_op jit(solution)/shard_map/all_to_all | solution.py:111
  265.7 4.2 %reshape.105 = bf16[576,1536]{1,0:T(8,128)(2,1)} reshape(bf16[64,9,1536]{2,1,0:T(8,128)(2,1)} %all-to-all-done.4) | data formatting | bytes 3538944 | tf_op jit(solution)/shard_map/reshape | solution.py:118
  270.0 2.7 fusion.13
  (48 shorter events, 11.6 us)
Async XLA Ops:
  0.0 179.6 %copy-start = (bf16[1,1536,1024]{2,1,0:T(8,128)(2,1)S(1)}, bf16[1,1536,1024]{2,1,0:T(8,128)(2,1)}, u32[]{:S(2)}) copy-start(bf16[1,1536,1024]{2,1,0:T(8,128)(2,1)} %param.20) | copy-start | bytes 9437188
  0.0 7.1 %copy-start.2 = (bf16[1,64,1024]{2,1,0:T(8,128)(2,1)S(1)}, bf16[1,64,1024]{2,1,0:T(8,128)(2,1)}, u32[]{:S(2)}) copy-start(bf16[1,64,1024]{2,1,0:T(8,128)(2,1)} %param.13) | copy-start | bytes 393220
  2.0 16.9 %all-to-all-start = ((bf16[4,64,1536]{2,1,0:T(8,128)(2,1)}), bf16[4,64,1536]{2,1,0:T(8,128)(2,1)}, u32[]{:S(2)}, u32[]{:S(2)}) async-start(bf16[4,64,1536]{2,1,0:T(8,128)(2,1)} %stack.12), calls=%async_computation | async-start | bytes 1572864 | tf_op jit(solution)/shard_map/all_to_all | solution.py:34
  10.2 4.8 %copy-start.3 = (s32[1,64,6]{1,0,2:T(1,128)S(1)}, s32[1,64,6]{1,0,2:T(1,128)}, u32[]{:S(2)}) copy-start(s32[1,64,6]{1,0,2:T(1,128)} %param.18) | copy-start | bytes 4612
  39.8 18.2 %all-to-all-start.1 = ((f32[4,1,1536]{2,1,0:T(1,128)}), f32[4,1,1536]{2,1,0:T(1,128)S(1)}, u32[]{:S(2)}, u32[]{:S(2)}) async-start(f32[4,1,1536]{2,1,0:T(1,128)} %reshape.112), calls=%async_computation.1 | async-start | bytes 49152 | tf_op jit(solution)/shard_map/all_to_all | solution.py:68
  58.0 24.4 %all-to-all-start.2 = ((f32[4,64,12,128]{3,1,2,0:T(8,128)}), f32[4,64,12,128]{3,1,2,0:T(8,128)}, u32[]{:S(2)}, u32[]{:S(2)}) async-start(f32[4,64,12,128]{3,1,2,0:T(8,128)} %copy.123), calls=%async_computation.2 | async-start | bytes 3145728 | tf_op jit(solution)/shard_map/all_to_all | solution.py:67
  84.3 3.5 %copy-start.1 = (pred[576,64]{0,1:T(8,128)(4,1)S(1)}, pred[576,64]{0,1:T(8,128)(4,1)}, u32[]{:S(2)}) copy-start(pred[576,64]{0,1:T(8,128)(4,1)} %fusion.28) | copy-start | bytes 110596
  84.3 3.5 %copy-start.4 = (f32[1536]{0:T(1024)S(1)}, f32[1536]{0:T(1024)}, u32[]{:S(2)}) copy-start(f32[1536]{0:T(1024)} %param.17) | copy-start | bytes 18436
  179.6 2.5 copy-start.6
  186.1 6.0 %copy-start.5 = (bf16[1,64,6]{1,2,0:T(8,128)(2,1)S(1)}, bf16[1,64,6]{1,2,0:T(8,128)(2,1)}, u32[]{:S(2)}) copy-start(bf16[1,64,6]{1,2,0:T(8,128)(2,1)} %param.19) | copy-start | bytes 2308
  186.1 79.6 %all-to-all-start.4 = ((bf16[64,9,1536]{2,1,0:T(8,128)(2,1)}), bf16[64,9,1536]{2,1,0:T(8,128)(2,1)}, u32[]{:S(2)}, u32[]{:S(2)}) async-start(bf16[64,9,1536]{2,1,0:T(8,128)(2,1)} %copy.132), calls=%async_computation.4 | async-start | bytes 6291456 | tf_op jit(solution)/shard_map/all_to_all | solution.py:111
